TPU v7x, 32 devices: a whole 2x2x4 slice. The times are simulated.
32 devices in a mesh: groups: 2 (over y), seq: 4 (over z), wloop: 2 (over x), heads: 2 (over core).
Axes of the slice: x: 2, y: 2, z: 4, core: 2. Of those that a mesh axis runs over, the one named last changes fastest.
Arguments:
- activations: bfloat16 [4, 2048, 2048], P(('groups', 'wloop'), 'seq'), parts along dimension 0, may hold values from -6 to 6
- norm_gain: float32 [2048], replicated, may hold values from 0.1 to 1.9
- w_query: bfloat16 [2048, 2048], P('wloop', 'heads'), may hold values from -0.125 to 0.125
- w_keyvalue: bfloat16 [2048, 2, 2048], P('wloop', None, 'heads'), may hold values from -0.125 to 0.125
- w_output: bfloat16 [2048, 2048], P('heads', 'wloop'), may hold values from -0.125 to 0.125
- log_retain: float32 [4, 16, 2048], P(('groups', 'wloop'), 'heads', 'seq'), parts along dimension 0, may hold values from -3 to 0, as said below
- resets: int32 [4, 4], P(('groups', 'wloop'), 'seq'), parts along dimension 0, may hold values 0 or 1
Outputs:
- layer_out: bfloat16 [4, 2048, 2048], P(('groups', 'wloop'), 'seq', 'heads'), parts along dimension 0
There are 2 independent parts, one for each index of `groups`. A program takes and returns all parts, laid end to end along the dimension named above; an argument that names none is the same for every part. Nothing has to cross between parts.
Inputs may be any that keep to these rules, and one draw needn't show every extreme that they name: `log_retain`: log retention per token and head, never above zero.
All inputs are finite; a program needn't handle non-finite values. No bound on the sum of `resets` on one device may be relied on, other than what follows from the above.
Results may differ from a plain program's by a relative error of at most 0.02.
Values may be sent and summed in bfloat16 or wider, within the bound.
No kernel may reach another device: no remote copies, remote signals or barrier semaphores. Data moves between devices by JAX's collectives and lax.ppermute only.
A program may use at most 128 MiB of HBM per device.

v0:
```python
import math
import jax
import jax.numpy as jnp
from jax import lax
from jax.sharding import PartitionSpec as P

SCORE_SCALE = 2.0


def shifted(value, axis, steps):
    count = lax.axis_size(axis)
    initial, last = (max(0, -steps), min(count, count - steps))
    return lax.ppermute(value, axis, [(source, source + steps) for source in range(initial, last)])


def rms_rows(values, eps):
    return values * lax.rsqrt(jnp.mean(values * values, axis=-1, keepdims=True) + eps)


def window_mix(queries, lookup_vectors, values, prior_keys, prior_values, allow, scale):
    own = (
        jnp.einsum("bihd,bjhd->bhij", queries, lookup_vectors, preferred_element_type=jnp.float32)
        * scale
    )
    prior = (
        jnp.einsum("bihd,bjhd->bhij", queries, prior_keys, preferred_element_type=jnp.float32)
        * scale
    )
    span = queries.shape[1]
    row_pos = lax.broadcasted_iota(jnp.int32, (span, span), 0)
    column_pos = lax.broadcasted_iota(jnp.int32, (span, span), 1)
    own_w = jnp.where(column_pos <= row_pos, jnp.exp(own), 0.0)
    prior_w = jnp.where((column_pos > row_pos) & allow[:, None, None, None], jnp.exp(prior), 0.0)
    total = jnp.sum(own_w, axis=-1, keepdims=True) + jnp.sum(prior_w, axis=-1, keepdims=True)
    own_p = (own_w / total).astype(jnp.bfloat16)
    prior_p = (prior_w / total).astype(jnp.bfloat16)
    return jnp.einsum(
        "bhij,bjhd->bihd", own_p, values, preferred_element_type=jnp.float32
    ) + jnp.einsum("bhij,bjhd->bihd", prior_p, prior_values, preferred_element_type=jnp.float32)


def shards(activations, norm_gain, w_query, w_keyvalue, w_output, log_retain, resets):
    trajs, span, width = activations.shape
    heads_here = log_retain.shape[1]
    inner_here = w_query.shape[1]
    head_dim = inner_here // heads_here
    scale = SCORE_SCALE / math.sqrt(head_dim)
    count = trajs * span
    normed = (rms_rows(activations.astype(jnp.float32), 1e-05) * norm_gain).astype(jnp.bfloat16)
    normed = normed.reshape(count, width)
    columns = normed
    query_raw = jnp.dot(
        columns,
        lax.all_gather(w_query, "wloop", axis=0, tiled=True),
        preferred_element_type=jnp.float32,
    )
    columns = normed
    pair_raw = jnp.einsum(
        "td,dje->jte",
        columns,
        lax.all_gather(w_keyvalue, "wloop", axis=0, tiled=True),
        preferred_element_type=jnp.float32,
    )
    lookup_vectors = rms_rows(pair_raw[0].reshape(trajs, span, heads_here, head_dim), 1e-06).astype(
        jnp.bfloat16
    )
    values = pair_raw[1].reshape(trajs, span, heads_here, head_dim).astype(jnp.bfloat16)
    prior_keys, prior_values = shifted(
        (lookup_vectors.reshape(trajs, span, inner_here), values.reshape(trajs, span, inner_here)),
        "seq",
        1,
    )
    queries = rms_rows(query_raw.reshape(trajs, span, heads_here, head_dim), 1e-06).astype(
        jnp.bfloat16
    )
    keep = (1 - resets[:, 0]).astype(jnp.float32)
    climb = jnp.cumsum(log_retain, axis=-1)
    whole = climb[:, :, -1]
    factor = jnp.exp(whole) * keep[:, None]
    weight = jnp.exp(whole[:, :, None] - climb)
    local_state = jnp.einsum(
        "bht,bthd,bthe->bhde",
        weight,
        lookup_vectors.astype(jnp.float32),
        values.astype(jnp.float32),
        precision=lax.Precision.HIGHEST,
    )
    local_mass = jnp.sum(weight * weight, axis=-1)

    def relay_turn(turn, carry):
        state, mass = carry
        return (
            shifted(
                (factor[:, :, None, None] * state + local_state).astype(jnp.bfloat16), "seq", 1
            ).astype(jnp.float32),
            shifted((factor * factor * mass + local_mass).astype(jnp.bfloat16), "seq", 1).astype(
                jnp.float32
            ),
        )

    entering, entering_mass = lax.fori_loop(
        0,
        lax.axis_size("seq") - 1,
        relay_turn,
        (jnp.zeros_like(local_state), jnp.zeros_like(local_mass)),
    )
    entering = entering * keep[:, None, None, None]
    entering_mass = entering_mass * keep[:, None]
    read = jnp.einsum(
        "bthd,bhde->bthe", queries.astype(jnp.float32), entering, precision=lax.Precision.HIGHEST
    )
    read = read * jnp.exp(climb).transpose(0, 2, 1)[..., None]
    read = read / jnp.sqrt(head_dim * (1.0 + entering_mass))[:, None, :, None]
    allow = (keep > 0.5) & (lax.axis_index("seq") > 0)
    window = window_mix(
        queries,
        lookup_vectors,
        values,
        prior_keys.reshape(trajs, span, heads_here, head_dim),
        prior_values.reshape(trajs, span, heads_here, head_dim),
        allow,
        scale,
    )
    attended = (window + read).astype(jnp.bfloat16).reshape(count, inner_here)
    partial_out = jnp.dot(
        attended,
        lax.all_gather(w_output, "wloop", axis=1, tiled=True),
        preferred_element_type=jnp.float32,
    )
    summed = lax.psum_scatter(
        partial_out.astype(jnp.bfloat16), "heads", scatter_dimension=1, tiled=True
    ).astype(jnp.float32)
    share = summed.shape[1]
    residual = lax.dynamic_slice_in_dim(
        activations.reshape(count, width), lax.axis_index("heads") * share, share, 1
    )
    return (residual.astype(jnp.float32) + summed).astype(jnp.bfloat16).reshape(trajs, span, share)


def solution(mesh):
    placed = (
        P(("groups", "wloop"), "seq", None),
        P(),
        P("wloop", "heads"),
        P("wloop", None, "heads"),
        P("heads", "wloop"),
        P(("groups", "wloop"), "heads", "seq"),
        P(("groups", "wloop"), "seq"),
    )
    return jax.shard_map(
        shards,
        mesh=mesh,
        in_specs=placed,
        out_specs=P(("groups", "wloop"), "seq", "heads"),
        check_vma=False,
    )
```

profile of v0, /device:TPU:0, one launch (start us, length us, event | category | flops | bytes accessed | tf_op | source)
XLA Modules:
  0.0 322.7 jit_solution(7021560980977442523)
XLA Ops:
  6.5 0.7 all-gather.6.cloned.1.call-update
  7.3 5.5 %copy.60 = bf16[1024,2,1024]{2,0,1:T(8,128)(2,1)} copy(bf16[1024,2,1024]{2,1,0:T(2,128)(2,1)} %param.12) | data formatting | bytes 8388608 | tf_op args[3]
  12.9 0.7 all-gather.8.cloned.1.call-update
  13.6 1.1 reduce-window.6
  16.2 0.8 iota_compare_fusion.1
  17.5 0.8 fusion.30
  18.3 50.1 %all-gather.6.cloned.1.call-done = bf16[2048,1024]{1,0:T(8,128)(2,1)} async-done(((bf16[1024,1024]{1,0:T(8,128)(2,1)}), bf16[2048,1024]{1,0:T(8,128)(2,1)}) %all-gather.6.cloned.1.call-update) | async-done | bytes 4194320 | tf_op jit(solution)/shard_map/all_gather | solution.py:54
  68.4 4.6 %fusion.18 = f32[512,1024]{1,0:T(8,128)S(1)} fusion(bf16[2048,1024]{1,0:T(8,128)(2,1)} %all-gather.6.cloned.1.call-done, bf16[1,512,2048]{2,1,0:T(8,128)(2,1)S(1)} %copy-done.2, f32[2048]{0:T(1024)S(1)} %copy-done.12, f32[512]{0:T(512)S(1)} %add_rsqrt_fusion.2), kind=kOutput, calls=%fused_computation.32 | convolution fusion | flops 2151677952 | bytes 8398848 | tf_op jit(solution)/shard_map/dot_general | solution.py:52
  73.2 1.1 copy-done.1
  74.7 0.6 reduce_sum.57
  75.5 3.2 fusion.12
  78.7 95.3 %all-gather.4.cloned.1.call-done = bf16[2048,2,1024]{2,0,1:T(8,128)(2,1)} async-done(((bf16[1024,2,1024]{2,0,1:T(8,128)(2,1)}), bf16[2048,2,1024]{2,0,1:T(8,128)(2,1)}) %all-gather.4.cloned.1.call-update) | async-done | bytes 8388624 | tf_op jit(solution)/shard_map/all_gather | solution.py:61
  173.9 6.9 %convolution_bitcast_fusion = f32[2,512,1024]{2,1,0:T(8,128)S(1)} fusion(bf16[2048,2,1024]{2,0,1:T(8,128)(2,1)} %all-gather.4.cloned.1.call-done, bf16[1,512,2048]{2,1,0:T(8,128)(2,1)S(1)} %copy-done.3, f32[2048]{0:T(1024)S(1)} %copy-done.12, f32[512]{0:T(512)S(1)} %add_rsqrt_fusion.2), kind=kOutput, calls=%fused_computation.21 | convolution fusion | flops 4299161600 | bytes 14690304 | tf_op jit(solution)/shard_map/td,dje->jte/dot_general | solution.py:58
  181.2 1.5 slice_bitcast_fusion.1
  182.7 0.6 copy-done
  183.3 1.2 slice.31
  185.7 1.6 mul.196
  187.3 2.1 copy.79
  189.4 3.9 %multiply_convert_fusion = (bf16[1,512,1024]{2,1,0:T(8,128)(2,1)}, f32[1,512,1024]{2,1,0:T(8,128)}) fusion(f32[1,512,1024]{2,1,0:T(8,128)S(1)} %copy.79, f32[2,512,1024]{2,1,0:T(8,128)} %copy-done), kind=kLoop, calls=%fused_computation.37 | loop fusion | flops 1048576 | bytes 7340032 | tf_op jit(solution)/shard_map/convert_element_type | solution.py:64
  193.2 1.9 copy.78
  195.1 1.5 copy.82
  196.7 4.4 %collective-permute-start.2 = (bf16[1,512,1024]{2,1,0:T(8,128)(2,1)}, bf16[1,512,1024]{2,1,0:T(8,128)(2,1)}, u32[]{:S(2)}, u32[]{:S(2)}) collective-permute-start(bf16[1,512,1024]{2,1,0:T(8,128)(2,1)} %get-tuple-element.111), channel_id=1, source_target_pairs={{0,4},{4,8},{8,12},{1,5},{5,9},{9,13},{2,6},{6,10},{10,14},{3,7},{... | collective-permute-start | bytes 3145736 | tf_op jit(solution)/shard_map/ppermute | solution.py:13
  201.0 3.5 %collective-permute-start.3 = (bf16[1,512,1024]{2,1,0:T(8,128)(2,1)}, bf16[1,512,1024]{2,1,0:T(8,128)(2,1)}, u32[]{:S(2)}, u32[]{:S(2)}) collective-permute-start(bf16[1,512,1024]{2,1,0:T(8,128)(2,1)} %slice.31), channel_id=1, source_target_pairs={{0,4},{4,8},{8,12},{1,5},{5,9},{9,13},{2,6},{6,10},{10,14},{3,7},{... | collective-permute-start | bytes 3145736 | tf_op jit(solution)/shard_map/ppermute | solution.py:13
  204.5 1.4 fusion.23
  205.9 64.6 %while.14 = (s32[]{:T(128)}, f32[1,8,128,128]{3,2,1,0:T(8,128)S(1)}, f32[1,8]{1,0:T(1,128)S(1)}, f32[1,8]{1,0:T(1,128)S(1)}, f32[1,8,128,128]{3,2,1,0:T(8,128)S(...) while((s32[]{:T(128)}, f32[1,8,128,128]{3,2,1,0:T(8,128)S(1)}, ...), condition=%wide.region_9.10_spmd.clone, body=%wide.region_8.9_spmd.clone.sunk | while | flops 655403 | bytes 3146168 | solution.py:101
  206.1 0.8 fusion.58
  206.9 2.3 collective-permute-start
  209.3 1.9 collective-permute-start.1
  211.2 39.4 %collective-permute-done.1 = bf16[1,8]{1,0:T(2,128)(2,1)S(1)} collective-permute-done((bf16[1,8]{1,0:T(2,128)(2,1)S(1)}, bf16[1,8]{1,0:T(2,128)(2,1)S(1)}, u32[]{:S(2)}, u32[]{:S(2)}) %collective-permute-start.1) | collective-permute-done | bytes 48 | tf_op jit(solution)/shard_map/while/body/eval_jaxpr/ppermute | solution.py:13
  250.6 0.8 fusion.58
  251.5 4.4 %collective-permute-start = (bf16[1,8,128,128]{3,2,1,0:T(8,128)(2,1)}, bf16[1,8,128,128]{3,2,1,0:T(8,128)(2,1)S(1)}, u32[]{:S(2)}, u32[]{:S(2)}) collective-permute-start(bf16[1,8,128,128]{3,2,1,0:T(8,128)(2,1)} %fusion.58), channel_id=1, source_target_pairs={{0,4},{4,8},{8,12},{1,5},{5,9},{9,13},{2,6},{6,10},{10,14},{3,7},{... | collective-permute-start | bytes 786440 | tf_op jit(solution)/shard_map/while/body/eval_jaxpr/ppermute | solution.py:13
  255.9 3.4 %collective-permute-start.1 = (bf16[1,8]{1,0:T(2,128)(2,1)S(1)}, bf16[1,8]{1,0:T(2,128)(2,1)S(1)}, u32[]{:S(2)}, u32[]{:S(2)}) collective-permute-start(bf16[1,8]{1,0:T(2,128)(2,1)S(1)} %fusion.59), channel_id=1, source_target_pairs={{0,4},{4,8},{8,12},{1,5},{5,9},{9,13},{2,6},{6,10},{10,14},{3,7},{... | collective-permute-start | bytes 56 | tf_op jit(solution)/shard_map/while/body/eval_jaxpr/ppermute | solution.py:13
  259.2 1.3 collective-permute-done.1
  260.6 0.8 fusion.58
  261.4 4.3 %collective-permute-start = (bf16[1,8,128,128]{3,2,1,0:T(8,128)(2,1)}, bf16[1,8,128,128]{3,2,1,0:T(8,128)(2,1)S(1)}, u32[]{:S(2)}, u32[]{:S(2)}) collective-permute-start(bf16[1,8,128,128]{3,2,1,0:T(8,128)(2,1)} %fusion.58), channel_id=1, source_target_pairs={{0,4},{4,8},{8,12},{1,5},{5,9},{9,13},{2,6},{6,10},{10,14},{3,7},{... | collective-permute-start | bytes 786440 | tf_op jit(solution)/shard_map/while/body/eval_jaxpr/ppermute | solution.py:13
  265.8 3.4 %collective-permute-start.1 = (bf16[1,8]{1,0:T(2,128)(2,1)S(1)}, bf16[1,8]{1,0:T(2,128)(2,1)S(1)}, u32[]{:S(2)}, u32[]{:S(2)}) collective-permute-start(bf16[1,8]{1,0:T(2,128)(2,1)S(1)} %fusion.59), channel_id=1, source_target_pairs={{0,4},{4,8},{8,12},{1,5},{5,9},{9,13},{2,6},{6,10},{10,14},{3,7},{... | collective-permute-start | bytes 56 | tf_op jit(solution)/shard_map/while/body/eval_jaxpr/ppermute | solution.py:13
  269.1 1.3 collective-permute-done.1
  270.5 3.7 %fusion.35 = f32[8,128,512]{2,1,0:T(8,128)} fusion(bf16[512,8,128]{2,0,1:T(8,128)(2,1)} %fusion.12, f32[1,8,128,128]{3,2,1,0:T(8,128)S(1)} %get-tuple-element.67, f32[]{:T(128)} %bitcast.16), kind=kOutput, calls=%fused_computation.51 | convolution fusion | flops 805437440 | bytes 3670020 | tf_op jit(solution)/shard_map/bthd,bhde->bthe/dot_general | solution.py:109
  274.2 5.5 %fusion.5 = (f32[8,512]{1,0:T(8,128)S(1)}, f32[8,512,512]{1,2,0:T(8,128)}) fusion(pred[512,512]{0,1:T(8,128)(4,1)S(1)} %copy-done.9, bf16[512,8,128]{2,0,1:T(8,128)(2,1)S(1)} %copy-done.7, f32[512,8,128]{0,2,1:T(8,128)S(1)} %bitcast.104, f32[512,8]{0,1:T(8,128)S(1)} %add_rsqrt_fusion), kind=kOutput, calls=%fused_computation.11 | convolution fusion | flops 544206848 | bytes 11829248 | tf_op jit(solution)/shard_map/bihd,bjhd->bhij/dot_general | solution.py:22
  279.7 1.5 copy.85
  281.2 5.2 %fusion.6 = (f32[8,512]{1,0:T(8,128)S(1)}, f32[8,512,512]{1,2,0:T(8,128)}) fusion(pred[512,512]{0,1:T(8,128)(4,1)S(1)} %copy-done.10, bf16[512,8,128]{2,0,1:T(8,128)(2,1)S(1)} %copy-done.7, bf16[512,8,128]{2,1,0:T(8,128)(2,1)S(1)} %bitcast.111), kind=kOutput, calls=%fused_computation.12 | convolution fusion | flops 543158272 | bytes 10764288 | tf_op jit(solution)/shard_map/bihd,bjhd->bhij/dot_general | solution.py:26
  286.5 1.6 copy.80
  288.1 4.8 %fusion.10 = f32[8,128,512]{2,1,0:T(8,128)S(1)} fusion(f32[8,512,512]{1,2,0:T(8,128)} %get-tuple-element.114, f32[8,512]{1,0:T(8,128)S(1)} %add.75, pred[512,512]{0,1:T(8,128)(4,1)S(1)} %copy-done.9, bf16[512,8,128]{2,1,0:T(8,128)(2,1)S(1)} %bitcast.109), kind=kOutput, calls=%fused_computation.18 | convolution fusion | flops 545259520 | bytes 11812864 | tf_op jit(solution)/shard_map/bhij,bjhd->bihd/dot_general | solution.py:37
  293.0 1.6 copy-done.13
  294.6 2.5 fusion.15
  297.1 5.9 %convolution_convert_fusion = bf16[512,2048]{1,0:T(8,128)(2,1)} fusion(bf16[512,1024]{0,1:T(8,128)(2,1)S(1)} %bitcast.117, bf16[1024,2048]{1,0:T(8,128)(2,1)} %all-gather.8.cloned.1.call-done), kind=kOutput, calls=%fused_computation.20 | convolution fusion | flops 2148532224 | bytes 7340032 | tf_op jit(solution)/shard_map/dot_general | solution.py:125
  303.1 10.5 %reduce-scatter.2.cloned.1.call-done = bf16[512,1024]{1,0:T(8,128)(2,1)} async-done(((bf16[512,2048]{1,0:T(8,128)(2,1)}), bf16[512,1024]{1,0:T(8,128)(2,1)}) %reduce-scatter.2.cloned.1.call-update) | async-done | bytes 1048592 | tf_op jit(solution)/shard_map/reduce_scatter | solution.py:130
  313.5 2.6 fusion.26
  (69 shorter events, 3.9 us)
Async XLA Ops:
  6.5 61.8 %all-gather.6.cloned.1.call-start = ((), (), s32[]{:S(2)}) async-start(), calls=%async_computation.2 | async-start | bytes 6291456 | tf_op jit(solution)/shard_map/all_gather | solution.py:54
  7.3 166.7 %all-gather.4.cloned.1.call-start = ((), (), s32[]{:S(2)}) async-start(), calls=%async_computation.1 | async-start | bytes 12582912 | tf_op jit(solution)/shard_map/all_gather | solution.py:61
  12.8 0.8 copy-start.11
  12.8 4.2 %copy-start.2 = (bf16[1,512,2048]{2,1,0:T(8,128)(2,1)S(1)}, bf16[1,512,2048]{2,1,0:T(8,128)(2,1)}, u32[]{:S(2)}) copy-start(bf16[1,512,2048]{2,1,0:T(8,128)(2,1)} %param.9) | copy-start | bytes 6291460
  12.8 55.5 %copy-start.12 = (f32[2048]{0:T(1024)S(1)}, f32[2048]{0:T(1024)}, u32[]{:S(2)}) copy-start(f32[2048]{0:T(1024)} %param.10) | copy-start | bytes 24580
  12.8 284.3 %all-gather.8.cloned.1.call-start = ((), (), s32[]{:S(2)}) async-start(), calls=%async_computation.3 | async-start | bytes 6291456 | tf_op jit(solution)/shard_map/all_gather | solution.py:127
  13.6 300.0 %reduce-scatter.2.cloned.1.call-start = ((), (), s32[]{:S(2)}) async-start(), calls=%async_computation.4 | async-start | bytes 3145728 | tf_op jit(solution)/shard_map/reduce_scatter | solution.py:130
  72.9 1.3 copy-start.1
  75.3 98.6 %copy-start.3 = (bf16[1,512,2048]{2,1,0:T(8,128)(2,1)S(1)}, bf16[1,512,2048]{2,1,0:T(8,128)(2,1)}, u32[]{:S(2)}) copy-start(bf16[1,512,2048]{2,1,0:T(8,128)(2,1)} %param.9) | copy-start | bytes 6291460
  180.9 2.5 copy-start
  196.6 7.9 %copy-start.5 = (bf16[64,8,8,128]{3,2,1,0:T(8,128)(2,1)}, bf16[64,8,8,128]{3,2,1,0:T(8,128)(2,1)S(1)}, u32[]{:S(2)}) copy-start(bf16[64,8,8,128]{3,2,1,0:T(8,128)(2,1)S(1)} %copy.82) | copy-start | bytes 3145732
  196.7 83.0 %collective-permute-start.2 = (bf16[1,512,1024]{2,1,0:T(8,128)(2,1)}, bf16[1,512,1024]{2,1,0:T(8,128)(2,1)}, u32[]{:S(2)}, u32[]{:S(2)}) collective-permute-start(bf16[1,512,1024]{2,1,0:T(8,128)(2,1)} %get-tuple-element.111), channel_id=1, source_target_pairs={{0,4},{4,8},{8,12},{1,5},{5,9},{9,13},{2,6},{6,10},{10,14},{3,7},{... | collective-permute-start | bytes 3145736 | tf_op jit(solution)/shard_map/ppermute | solution.py:13
  201.0 85.5 %collective-permute-start.3 = (bf16[1,512,1024]{2,1,0:T(8,128)(2,1)}, bf16[1,512,1024]{2,1,0:T(8,128)(2,1)}, u32[]{:S(2)}, u32[]{:S(2)}) collective-permute-start(bf16[1,512,1024]{2,1,0:T(8,128)(2,1)} %slice.31), channel_id=1, source_target_pairs={{0,4},{4,8},{8,12},{1,5},{5,9},{9,13},{2,6},{6,10},{10,14},{3,7},{... | collective-permute-start | bytes 3145736 | tf_op jit(solution)/shard_map/ppermute | solution.py:13
  206.9 43.7 %collective-permute-start = (bf16[1,8,128,128]{3,2,1,0:T(8,128)(2,1)}, bf16[1,8,128,128]{3,2,1,0:T(8,128)(2,1)S(1)}, u32[]{:S(2)}, u32[]{:S(2)}) collective-permute-start(bf16[1,8,128,128]{3,2,1,0:T(8,128)(2,1)} %fusion.58), channel_id=1, source_target_pairs={{0,4},{4,8},{8,12},{1,5},{5,9},{9,13},{2,6},{6,10},{10,14},{3,7},{... | collective-permute-start | bytes 786440 | tf_op jit(solution)/shard_map/while/body/eval_jaxpr/ppermute | solution.py:13
  209.3 41.3 %collective-permute-start.1 = (bf16[1,8]{1,0:T(2,128)(2,1)S(1)}, bf16[1,8]{1,0:T(2,128)(2,1)S(1)}, u32[]{:S(2)}, u32[]{:S(2)}) collective-permute-start(bf16[1,8]{1,0:T(2,128)(2,1)S(1)} %fusion.59), channel_id=1, source_target_pairs={{0,4},{4,8},{8,12},{1,5},{5,9},{9,13},{2,6},{6,10},{10,14},{3,7},{... | collective-permute-start | bytes 56 | tf_op jit(solution)/shard_map/while/body/eval_jaxpr/ppermute | solution.py:13
  251.5 9.1 %collective-permute-start = (bf16[1,8,128,128]{3,2,1,0:T(8,128)(2,1)}, bf16[1,8,128,128]{3,2,1,0:T(8,128)(2,1)S(1)}, u32[]{:S(2)}, u32[]{:S(2)}) collective-permute-start(bf16[1,8,128,128]{3,2,1,0:T(8,128)(2,1)} %fusion.58), channel_id=1, source_target_pairs={{0,4},{4,8},{8,12},{1,5},{5,9},{9,13},{2,6},{6,10},{10,14},{3,7},{... | collective-permute-start | bytes 786440 | tf_op jit(solution)/shard_map/while/body/eval_jaxpr/ppermute | solution.py:13
  255.9 4.7 %collective-permute-start.1 = (bf16[1,8]{1,0:T(2,128)(2,1)S(1)}, bf16[1,8]{1,0:T(2,128)(2,1)S(1)}, u32[]{:S(2)}, u32[]{:S(2)}) collective-permute-start(bf16[1,8]{1,0:T(2,128)(2,1)S(1)} %fusion.59), channel_id=1, source_target_pairs={{0,4},{4,8},{8,12},{1,5},{5,9},{9,13},{2,6},{6,10},{10,14},{3,7},{... | collective-permute-start | bytes 56 | tf_op jit(solution)/shard_map/while/body/eval_jaxpr/ppermute | solution.py:13
  261.4 9.0 %collective-permute-start = (bf16[1,8,128,128]{3,2,1,0:T(8,128)(2,1)}, bf16[1,8,128,128]{3,2,1,0:T(8,128)(2,1)S(1)}, u32[]{:S(2)}, u32[]{:S(2)}) collective-permute-start(bf16[1,8,128,128]{3,2,1,0:T(8,128)(2,1)} %fusion.58), channel_id=1, source_target_pairs={{0,4},{4,8},{8,12},{1,5},{5,9},{9,13},{2,6},{6,10},{10,14},{3,7},{... | collective-permute-start | bytes 786440 | tf_op jit(solution)/shard_map/while/body/eval_jaxpr/ppermute | solution.py:13
  265.8 4.7 %collective-permute-start.1 = (bf16[1,8]{1,0:T(2,128)(2,1)S(1)}, bf16[1,8]{1,0:T(2,128)(2,1)S(1)}, u32[]{:S(2)}, u32[]{:S(2)}) collective-permute-start(bf16[1,8]{1,0:T(2,128)(2,1)S(1)} %fusion.59), channel_id=1, source_target_pairs={{0,4},{4,8},{8,12},{1,5},{5,9},{9,13},{2,6},{6,10},{10,14},{3,7},{... | collective-permute-start | bytes 56 | tf_op jit(solution)/shard_map/while/body/eval_jaxpr/ppermute | solution.py:13
  270.5 3.7 %copy-start.7 = (bf16[512,8,128]{2,0,1:T(8,128)(2,1)S(1)}, bf16[512,8,128]{2,0,1:T(8,128)(2,1)}, u32[]{:S(2)}) copy-start(bf16[512,8,128]{2,0,1:T(8,128)(2,1)} %fusion.12) | copy-start | bytes 3145732
  270.5 3.7 %copy-start.9 = (pred[512,512]{0,1:T(8,128)(4,1)S(1)}, pred[512,512]{0,1:T(8,128)(4,1)}, u32[]{:S(2)}) copy-start(pred[512,512]{0,1:T(8,128)(4,1)} %iota_compare_fusion.1) | copy-start | bytes 786436
  279.7 1.5 copy-start.10
  286.5 1.6 copy-start.6
  288.1 4.9 %copy-start.8 = (f32[8,128,512]{2,1,0:T(8,128)S(1)}, f32[8,128,512]{2,1,0:T(8,128)}, u32[]{:S(2)}) copy-start(f32[8,128,512]{2,1,0:T(8,128)} %fusion.35) | copy-start | bytes 6291460
  288.1 6.5 %copy-start.13 = (f32[8,512,512]{1,2,0:T(8,128)S(1)}, f32[8,512,512]{1,2,0:T(8,128)}, u32[]{:S(2)}) copy-start(f32[8,512,512]{1,2,0:T(8,128)} %get-tuple-element.116) | copy-start | bytes 25165828
  303.0 10.5 %copy-start.4 = (bf16[1,512,2048]{2,1,0:T(8,128)(2,1)S(1)}, bf16[1,512,2048]{2,1,0:T(8,128)(2,1)}, u32[]{:S(2)}) copy-start(bf16[1,512,2048]{2,1,0:T(8,128)(2,1)} %param.9) | copy-start | bytes 6291460
Sparse Core Ops, SparseCore 0:
  8.9 59.4 all-gather.5
  69.9 103.9 all-gather.3
  175.5 56.7 all-gather.7
  303.2 10.3 reduce-scatter.1
where the time goes:
time: 323 us
  waiting for transfers between devices  199 us (62%)
  matrix products  40.5 us (13%)
  starting transfers between devices  27.7 us (9%)
  local copies, waits for them, and re-layouts  23 us (7%)
  other arithmetic  17.9 us (6%)
  between operations  14.1 us (4%)
    all_gather x1, waiting for transfers between devices, shards(): lax.all_gather(w_keyvalue, 'wloop', axis=0, tiled=True)  95.3 us
    all_gather x1, waiting for transfers between devices, shards(): lax.all_gather(w_query, 'wloop', axis=0, tiled=True)  50.1 us
    ppermute x8, waiting for transfers between devices, shifted(): lax.ppermute(value, axis, [(source, source + steps) for source in range(i...  42 us
    ppermute x8, starting transfers between devices, shifted(): lax.ppermute(value, axis, [(source, source + steps) for source in range(i...  27.6 us
    unnamed x34, local copies, waits for them, and re-layouts  14.3 us
    reduce_scatter x1, waiting for transfers between devices, shards(): lax.psum_scatter(partial_out.astype(jnp.bfloat16), 'heads', scatter_dimen...  10.5 us
    dot_general x1, matrix products, shards(): jnp.einsum('td,dje->jte', columns, lax.all_gather(w_keyvalue, 'wloop', ax...  6.94 us
  transfers between devices with their start and end apart: 12, of which 6 were waited for; matrix products, arithmetic and copies ran while one was open for 22% of the time, Pallas kernels for 0%

commit v1 on v0

--- a/solution.py
+++ b/solution.py
@@ -5,6 +5,18 @@
 from jax.sharding import PartitionSpec as P
 
 SCORE_SCALE = 2.0
+
+
+def collect(x, axis, dim):
+    ways, here = (lax.axis_size(axis), lax.axis_index(axis))
+    grown, reach = (x, 1)
+    while reach < ways:
+        theirs = lax.ppermute(grown, axis, [(d, d ^ reach) for d in range(ways)])
+        mine_first = jnp.concatenate([grown, theirs], axis=dim)
+        theirs_first = jnp.concatenate([theirs, grown], axis=dim)
+        grown = jnp.where(here & reach == 0, mine_first, theirs_first)
+        reach = 2 * reach
+    return grown
 
 
 def shifted(value, axis, steps):
@@ -56,10 +68,7 @@
     )
     columns = normed
     pair_raw = jnp.einsum(
-        "td,dje->jte",
-        columns,
-        lax.all_gather(w_keyvalue, "wloop", axis=0, tiled=True),
-        preferred_element_type=jnp.float32,
+        "td,dje->jte", columns, collect(w_keyvalue, "wloop", 0), preferred_element_type=jnp.float32
     )
     lookup_vectors = rms_rows(pair_raw[0].reshape(trajs, span, heads_here, head_dim), 1e-06).astype(
         jnp.bfloat16

time: 323 us -> 349 us (1.080)
  other arithmetic: 17.9 us -> 58.5 us
  local copies, waits for them, and re-layouts: 23 us -> 5.04 us
  matrix products: 40.5 us -> 36.4 us
  waiting for transfers between devices: 199 us -> 203 us
  starting transfers between devices: 27.7 us -> 31.2 us
    ppermute x0 -> x1, waiting for transfers between devices: none -> 152 us  [collect(): theirs = lax.ppermute(grown, axis, [(d, d ^ reach) for d in range(ways)])]
    all_gather x1 -> x0, waiting for transfers between devices: 95.3 us -> none  [shards(): lax.all_gather(w_keyvalue, 'wloop', axis=0, tiled=True)]
    all_gather x1, waiting for transfers between devices: 50.1 us -> 0.01 us  [shards(): lax.all_gather(w_query, 'wloop', axis=0, tiled=True)]
    select_n x0 -> x1, other arithmetic: none -> 40.8 us  [collect(): grown = jnp.where(here & reach == 0, mine_first, theirs_first)]
    unnamed x34 -> x21, local copies, waits for them, and re-layouts: 14.3 us -> 3.6 us
    ppermute x8, waiting for transfers between devices: 42 us -> 37.7 us  [shifted(): lax.ppermute(value, axis, [(source, source + steps) for source in range(i...]
    mul x2 -> x0, local copies, waits for them, and re-layouts: 3.66 us -> none  [rms_rows(): values * lax.rsqrt(jnp.mean(values * values, axis=-1, keepdims=True) + eps)]
    another operation x3 -> x1, local copies, waits for them, and re-layouts: 3.51 us -> 0.01 us  [the longest x1 1.92 us: shards(): pair_raw[0].reshape(trajs, span, heads_here, head_dim)]
  transfers between devices with their start and end apart: 12 -> 12, of which waited for: 6 -> 5; matrix products, arithmetic and copies ran while one was open for 22% -> 26% of each run, Pallas kernels for 0% -> 0%
where the time goes in v1:
time: 349 us; the launch traced here: 348 us
  waiting for transfers between devices  203 us (58%)
  other arithmetic  58.5 us (17%)
  matrix products  36.4 us (10%)
  starting transfers between devices  31.2 us (9%)
  between operations  14.1 us (4%)
  local copies, waits for them, and re-layouts  5.04 us (1%)
    ppermute x1, waiting for transfers between devices, collect(): theirs = lax.ppermute(grown, axis, [(d, d ^ reach) for d in range(ways)])  152 us
    select_n x1, other arithmetic, collect(): grown = jnp.where(here & reach == 0, mine_first, theirs_first)  40.8 us
    ppermute x8, waiting for transfers between devices, shifted(): lax.ppermute(value, axis, [(source, source + steps) for source in range(i...  37.7 us
    ppermute x8, starting transfers between devices, shifted(): lax.ppermute(value, axis, [(source, source + steps) for source in range(i...  28.1 us
    reduce_scatter x1, waiting for transfers between devices, shards(): lax.psum_scatter(partial_out.astype(jnp.bfloat16), 'heads', scatter_dimen...  11.9 us
  transfers between devices with their start and end apart: 12, of which 5 were waited for; matrix products, arithmetic and copies ran while one was open for 26% of the time, Pallas kernels for 0%

profile of v1, /device:TPU:0, one launch (start us, length us, event | category | flops | bytes accessed | tf_op | source)
XLA Modules:
  0.0 348.3 jit_solution(6438321990390702139)
XLA Ops:
  6.5 0.7 all-gather.3.cloned.1.call-update
  7.3 3.0 collective-permute-start.2
  10.4 1.1 reduce-window.6
  11.6 0.2 slice_reduce_fusion
  12.5 0.2 slice_reduce_fusion.1
  12.7 0.2 multiply_reduce_fusion
  12.9 0.8 iota_compare_fusion.1
  13.7 0.8 fusion.34
  14.5 0.5 fusion.9
  15.0 0.1 fusion.44
  15.1 152.4 %collective-permute-done.2 = bf16[1024,2,1024]{2,1,0:T(2,128)(2,1)} collective-permute-done((bf16[1024,2,1024]{2,1,0:T(2,128)(2,1)}, bf16[1024,2,1024]{2,1,0:T(2,128)(2,1)}, u32[]{:S(2)}, u32[]{:S(2)}) %collective-permute-start.2) | collective-permute-done | bytes 4194336 | tf_op jit(solution)/shard_map/ppermute | solution.py:14
  167.5 40.8 %broadcast_select_fusion.1 = bf16[2048,2,1024]{2,1,0:T(2,128)(2,1)S(1)} fusion(pred[]{:T(512)S(6)} %eq.3, bf16[1024,2,1024]{2,1,0:T(2,128)(2,1)} %collective-permute-done.2, bf16[1024,2,1024]{2,1,0:T(2,128)(2,1)} %param.12), kind=kLoop, calls=%fused_computation.7 | loop fusion | flops 12582912 | bytes 16777216 | tf_op jit(solution)/shard_map/jit(_where)/select_n | solution.py:17
  208.3 5.7 %fusion.14 = f32[2,512,1024]{1,2,0:T(8,128)S(1)} fusion(bf16[2048,2,1024]{2,1,0:T(2,128)(2,1)S(1)} %broadcast_select_fusion.1, bf16[1,512,2048]{2,1,0:T(8,128)(2,1)S(1)} %copy-done.2, f32[2048]{0:T(1024)S(1)} %copy-done.9, f32[512]{0:T(512)S(1)} %add_rsqrt_fusion.2), kind=kOutput, calls=%fused_computation.24 | convolution fusion | flops 4299161600 | bytes 14690304 | tf_op jit(solution)/shard_map/td,dje->jte/dot_general | solution.py:70
  214.0 0.2 slice_multiply_fusion
  214.3 1.7 copy-done.1
  216.0 1.2 slice.31
  217.2 0.2 reduce_sum.58
  217.4 3.0 fusion.22
  220.4 5.2 %fusion.24 = f32[512,1024]{1,0:T(8,128)S(1)} fusion(bf16[2048,1024]{1,0:T(8,128)(2,1)} %all-gather.3.cloned.1.call-done, bf16[1,512,2048]{2,1,0:T(8,128)(2,1)} %param.9, f32[2048]{0:T(1024)S(1)} %copy-done.9, f32[512]{0:T(512)S(1)} %add_rsqrt_fusion.2), kind=kOutput, calls=%fused_computation.37 | convolution fusion | flops 2151677952 | bytes 8398848 | tf_op jit(solution)/shard_map/dot_general | solution.py:64
  225.6 0.3 multiply_bitcast_fusion
  225.9 1.8 copy.71
  227.7 2.2 reduce_sum.57
  229.9 0.1 copy.56
  230.1 2.7 fusion.17
  232.8 4.4 %collective-permute-start.3 = (bf16[1,512,1024]{1,2,0:T(8,128)(2,1)}, bf16[1,512,1024]{1,2,0:T(8,128)(2,1)}, u32[]{:S(2)}, u32[]{:S(2)}) collective-permute-start(bf16[1,512,1024]{1,2,0:T(8,128)(2,1)} %get-tuple-element.111), channel_id=1, source_target_pairs={{0,4},{4,8},{8,12},{1,5},{5,9},{9,13},{2,6},{6,10},{10,14},{3,7},{... | collective-permute-start | bytes 3145736 | tf_op jit(solution)/shard_map/ppermute | solution.py:25
  237.2 3.5 %collective-permute-start.4 = (bf16[1,512,1024]{1,2,0:T(8,128)(2,1)}, bf16[1,512,1024]{1,2,0:T(8,128)(2,1)}, u32[]{:S(2)}, u32[]{:S(2)}) collective-permute-start(bf16[1,512,1024]{1,2,0:T(8,128)(2,1)} %slice.31), channel_id=1, source_target_pairs={{0,4},{4,8},{8,12},{1,5},{5,9},{9,13},{2,6},{6,10},{10,14},{3,7},{... | collective-permute-start | bytes 3145736 | tf_op jit(solution)/shard_map/ppermute | solution.py:25
  240.7 2.4 fusion.29
  243.1 60.8 %while.14 = (s32[]{:T(128)}, f32[1,8,128,128]{3,2,1,0:T(8,128)S(1)}, f32[1,8]{1,0:T(1,128)S(1)}, f32[1,8]{1,0:T(1,128)S(1)}, f32[1,8,128,128]{3,2,1,0:T(8,128)S(...) while((s32[]{:T(128)}, f32[1,8,128,128]{3,2,1,0:T(8,128)S(1)}, ...), condition=%wide.region_9.10_spmd.clone, body=%wide.region_8.9_spmd.clone.sunk | while | flops 655403 | bytes 3146168 | solution.py:110
  243.4 0.8 fusion.62
  244.2 2.6 collective-permute-start
  246.8 1.9 collective-permute-start.1
  248.7 35.1 %collective-permute-done.1 = bf16[1,8]{1,0:T(2,128)(2,1)S(1)} collective-permute-done((bf16[1,8]{1,0:T(2,128)(2,1)S(1)}, bf16[1,8]{1,0:T(2,128)(2,1)S(1)}, u32[]{:S(2)}, u32[]{:S(2)}) %collective-permute-start.1) | collective-permute-done | bytes 48 | tf_op jit(solution)/shard_map/while/body/eval_jaxpr/ppermute | solution.py:25
  283.9 0.8 fusion.62
  284.7 4.4 %collective-permute-start = (bf16[1,8,128,128]{3,2,1,0:T(8,128)(2,1)}, bf16[1,8,128,128]{3,2,1,0:T(8,128)(2,1)S(1)}, u32[]{:S(2)}, u32[]{:S(2)}) collective-permute-start(bf16[1,8,128,128]{3,2,1,0:T(8,128)(2,1)} %fusion.62), channel_id=1, source_target_pairs={{0,4},{4,8},{8,12},{1,5},{5,9},{9,13},{2,6},{6,10},{10,14},{3,7},{... | collective-permute-start | bytes 786440 | tf_op jit(solution)/shard_map/while/body/eval_jaxpr/ppermute | solution.py:25
  289.1 3.6 %collective-permute-start.1 = (bf16[1,8]{1,0:T(2,128)(2,1)S(1)}, bf16[1,8]{1,0:T(2,128)(2,1)S(1)}, u32[]{:S(2)}, u32[]{:S(2)}) collective-permute-start(bf16[1,8]{1,0:T(2,128)(2,1)S(1)} %fusion.63), channel_id=1, source_target_pairs={{0,4},{4,8},{8,12},{1,5},{5,9},{9,13},{2,6},{6,10},{10,14},{3,7},{... | collective-permute-start | bytes 56 | tf_op jit(solution)/shard_map/while/body/eval_jaxpr/ppermute | solution.py:25
  292.7 1.3 collective-permute-done.1
  294.0 0.8 fusion.62
  294.9 4.2 %collective-permute-start = (bf16[1,8,128,128]{3,2,1,0:T(8,128)(2,1)}, bf16[1,8,128,128]{3,2,1,0:T(8,128)(2,1)S(1)}, u32[]{:S(2)}, u32[]{:S(2)}) collective-permute-start(bf16[1,8,128,128]{3,2,1,0:T(8,128)(2,1)} %fusion.62), channel_id=1, source_target_pairs={{0,4},{4,8},{8,12},{1,5},{5,9},{9,13},{2,6},{6,10},{10,14},{3,7},{... | collective-permute-start | bytes 786440 | tf_op jit(solution)/shard_map/while/body/eval_jaxpr/ppermute | solution.py:25
  299.1 3.6 %collective-permute-start.1 = (bf16[1,8]{1,0:T(2,128)(2,1)S(1)}, bf16[1,8]{1,0:T(2,128)(2,1)S(1)}, u32[]{:S(2)}, u32[]{:S(2)}) collective-permute-start(bf16[1,8]{1,0:T(2,128)(2,1)S(1)} %fusion.63), channel_id=1, source_target_pairs={{0,4},{4,8},{8,12},{1,5},{5,9},{9,13},{2,6},{6,10},{10,14},{3,7},{... | collective-permute-start | bytes 56 | tf_op jit(solution)/shard_map/while/body/eval_jaxpr/ppermute | solution.py:25
  302.6 1.3 collective-permute-done.1
  304.0 2.3 fusion.37
  306.3 3.8 %fusion.7 = (f32[8,512]{1,0:T(8,128)S(1)}, f32[8,512,512]{1,2,0:T(8,128)S(1)}) fusion(pred[512,512]{0,1:T(8,128)(4,1)} %iota_compare_fusion.1, bf16[512,8,128]{2,0,1:T(8,128)(2,1)} %fusion.17, f32[512,8,128]{0,2,1:T(8,128)S(1)} %bitcast.101, f32[512,8]{0,1:T(8,128)S(1)} %add_rsqrt_fusion), kind=kOutput, calls=%fused_computation.14 | convolution fusion | flops 544206848 | bytes 11829248 | tf_op jit(solution)/shard_map/bihd,bjhd->bhij/dot_general | solution.py:34
  310.2 3.7 %fusion.8 = (f32[8,512]{1,0:T(8,128)S(1)}, f32[8,512,512]{1,2,0:T(8,128)S(1)}) fusion(pred[512,512]{0,1:T(8,128)(4,1)S(1)} %copy-done.6, bf16[512,8,128]{2,0,1:T(8,128)(2,1)S(1)} %copy-done.5, bf16[512,8,128]{0,2,1:T(8,128)(2,1)} %bitcast.11), kind=kOutput, calls=%fused_computation.15 | convolution fusion | flops 543158272 | bytes 10764288 | tf_op jit(solution)/shard_map/bihd,bjhd->bhij/dot_general | solution.py:38
  313.9 2.4 fusion.12
  316.3 4.6 %fusion.20 = bf16[1,512,8,128]{1,3,2,0:T(8,128)(2,1)} fusion(f32[8,128,512]{2,1,0:T(8,128)S(1)} %fusion.37, f32[8,128,512]{2,1,0:T(8,128)S(1)} %fusion.12, bf16[512,8,128]{0,2,1:T(8,128)(2,1)} %bitcast.12, f32[8,512,512]{1,2,0:T(8,128)S(1)} %get-tuple-element.116, f32[8,512]{1,0:T(8,128)S(1)} %add.75, pred[512,512]{0,1:T(8,128)(4,1)S(1)} %copy-done.6, ...), kind=kOutput, calls=%fused_computation.31 | convolution fusion | flops 547880960 | bytes 14975008 | tf_op jit(solution)/shard_map/bhij,bjhd->bihd/dot_general | solution.py:51
  320.9 6.4 %convolution_convert_fusion = bf16[512,2048]{1,0:T(8,128)(2,1)} fusion(bf16[512,1024]{0,1:T(8,128)(2,1)} %bitcast.111, bf16[1024,2048]{1,0:T(8,128)(2,1)} %all-gather.5.cloned.1.call-done), kind=kOutput, calls=%fused_computation.23 | convolution fusion | flops 2148532224 | bytes 7340032 | tf_op jit(solution)/shard_map/dot_general | solution.py:134
  327.3 11.9 %reduce-scatter.2.cloned.1.call-done = bf16[512,1024]{1,0:T(8,128)(2,1)} async-done(((bf16[512,2048]{1,0:T(8,128)(2,1)}), bf16[512,1024]{1,0:T(8,128)(2,1)}) %reduce-scatter.2.cloned.1.call-update) | async-done | bytes 1048592 | tf_op jit(solution)/shard_map/reduce_scatter | solution.py:139
  339.2 2.6 fusion.32
  (51 shorter events, 0.5 us)
Async XLA Ops:
  6.5 3.9 %copy-start.8 = (f32[1,8,512]{2,1,0:T(8,128)S(1)}, f32[1,8,512]{2,1,0:T(8,128)}, u32[]{:S(2)}) copy-start(f32[1,8,512]{2,1,0:T(8,128)} %param.14) | copy-start | bytes 49156
  6.5 8.0 %copy-start.2 = (bf16[1,512,2048]{2,1,0:T(8,128)(2,1)S(1)}, bf16[1,512,2048]{2,1,0:T(8,128)(2,1)}, u32[]{:S(2)}) copy-start(bf16[1,512,2048]{2,1,0:T(8,128)(2,1)} %param.9) | copy-start | bytes 6291460
  6.5 213.9 %all-gather.3.cloned.1.call-start = ((), (), s32[]{:S(2)}) async-start(), calls=%async_computation.1 | async-start | bytes 6291456 | tf_op jit(solution)/shard_map/all_gather | solution.py:66
  7.3 313.6 %all-gather.5.cloned.1.call-start = ((), (), s32[]{:S(2)}) async-start(), calls=%async_computation.2 | async-start | bytes 6291456 | tf_op jit(solution)/shard_map/all_gather | solution.py:136
  7.3 160.2 %collective-permute-start.2 = (bf16[1024,2,1024]{2,1,0:T(2,128)(2,1)}, bf16[1024,2,1024]{2,1,0:T(2,128)(2,1)}, u32[]{:S(2)}, u32[]{:S(2)}) collective-permute-start(bf16[1024,2,1024]{2,1,0:T(2,128)(2,1)} %param.12), channel_id=1, source_target_pairs={{0,2},{2,0},{1,3},{3,1},{4,6},{6,4},{5,7},{7,5},{8,10},{10,8},{9,1... | collective-permute-start | bytes 12582920 | tf_op jit(solution)/shard_map/ppermute | solution.py:14
  10.4 328.8 %reduce-scatter.2.cloned.1.call-start = ((), (), s32[]{:S(2)}) async-start(), calls=%async_computation.3 | async-start | bytes 3145728 | tf_op jit(solution)/shard_map/reduce_scatter | solution.py:139
  15.1 193.2 %copy-start.9 = (f32[2048]{0:T(1024)S(1)}, f32[2048]{0:T(1024)}, u32[]{:S(2)}) copy-start(f32[2048]{0:T(1024)} %param.10) | copy-start | bytes 24580
  214.0 2.0 copy-start.1
  225.6 2.1 copy-start
  232.8 77.3 %collective-permute-start.3 = (bf16[1,512,1024]{1,2,0:T(8,128)(2,1)}, bf16[1,512,1024]{1,2,0:T(8,128)(2,1)}, u32[]{:S(2)}, u32[]{:S(2)}) collective-permute-start(bf16[1,512,1024]{1,2,0:T(8,128)(2,1)} %get-tuple-element.111), channel_id=1, source_target_pairs={{0,4},{4,8},{8,12},{1,5},{5,9},{9,13},{2,6},{6,10},{10,14},{3,7},{... | collective-permute-start | bytes 3145736 | tf_op jit(solution)/shard_map/ppermute | solution.py:25
  237.2 79.2 %collective-permute-start.4 = (bf16[1,512,1024]{1,2,0:T(8,128)(2,1)}, bf16[1,512,1024]{1,2,0:T(8,128)(2,1)}, u32[]{:S(2)}, u32[]{:S(2)}) collective-permute-start(bf16[1,512,1024]{1,2,0:T(8,128)(2,1)} %slice.31), channel_id=1, source_target_pairs={{0,4},{4,8},{8,12},{1,5},{5,9},{9,13},{2,6},{6,10},{10,14},{3,7},{... | collective-permute-start | bytes 3145736 | tf_op jit(solution)/shard_map/ppermute | solution.py:25
  244.2 39.6 %collective-permute-start = (bf16[1,8,128,128]{3,2,1,0:T(8,128)(2,1)}, bf16[1,8,128,128]{3,2,1,0:T(8,128)(2,1)S(1)}, u32[]{:S(2)}, u32[]{:S(2)}) collective-permute-start(bf16[1,8,128,128]{3,2,1,0:T(8,128)(2,1)} %fusion.62), channel_id=1, source_target_pairs={{0,4},{4,8},{8,12},{1,5},{5,9},{9,13},{2,6},{6,10},{10,14},{3,7},{... | collective-permute-start | bytes 786440 | tf_op jit(solution)/shard_map/while/body/eval_jaxpr/ppermute | solution.py:25
  246.8 37.0 %collective-permute-start.1 = (bf16[1,8]{1,0:T(2,128)(2,1)S(1)}, bf16[1,8]{1,0:T(2,128)(2,1)S(1)}, u32[]{:S(2)}, u32[]{:S(2)}) collective-permute-start(bf16[1,8]{1,0:T(2,128)(2,1)S(1)} %fusion.63), channel_id=1, source_target_pairs={{0,4},{4,8},{8,12},{1,5},{5,9},{9,13},{2,6},{6,10},{10,14},{3,7},{... | collective-permute-start | bytes 56 | tf_op jit(solution)/shard_map/while/body/eval_jaxpr/ppermute | solution.py:25
  284.7 9.2 %collective-permute-start = (bf16[1,8,128,128]{3,2,1,0:T(8,128)(2,1)}, bf16[1,8,128,128]{3,2,1,0:T(8,128)(2,1)S(1)}, u32[]{:S(2)}, u32[]{:S(2)}) collective-permute-start(bf16[1,8,128,128]{3,2,1,0:T(8,128)(2,1)} %fusion.62), channel_id=1, source_target_pairs={{0,4},{4,8},{8,12},{1,5},{5,9},{9,13},{2,6},{6,10},{10,14},{3,7},{... | collective-permute-start | bytes 786440 | tf_op jit(solution)/shard_map/while/body/eval_jaxpr/ppermute | solution.py:25
  289.1 4.8 %collective-permute-start.1 = (bf16[1,8]{1,0:T(2,128)(2,1)S(1)}, bf16[1,8]{1,0:T(2,128)(2,1)S(1)}, u32[]{:S(2)}, u32[]{:S(2)}) collective-permute-start(bf16[1,8]{1,0:T(2,128)(2,1)S(1)} %fusion.63), channel_id=1, source_target_pairs={{0,4},{4,8},{8,12},{1,5},{5,9},{9,13},{2,6},{6,10},{10,14},{3,7},{... | collective-permute-start | bytes 56 | tf_op jit(solution)/shard_map/while/body/eval_jaxpr/ppermute | solution.py:25
  294.9 9.1 %collective-permute-start = (bf16[1,8,128,128]{3,2,1,0:T(8,128)(2,1)}, bf16[1,8,128,128]{3,2,1,0:T(8,128)(2,1)S(1)}, u32[]{:S(2)}, u32[]{:S(2)}) collective-permute-start(bf16[1,8,128,128]{3,2,1,0:T(8,128)(2,1)} %fusion.62), channel_id=1, source_target_pairs={{0,4},{4,8},{8,12},{1,5},{5,9},{9,13},{2,6},{6,10},{10,14},{3,7},{... | collective-permute-start | bytes 786440 | tf_op jit(solution)/shard_map/while/body/eval_jaxpr/ppermute | solution.py:25
  299.1 4.8 %collective-permute-start.1 = (bf16[1,8]{1,0:T(2,128)(2,1)S(1)}, bf16[1,8]{1,0:T(2,128)(2,1)S(1)}, u32[]{:S(2)}, u32[]{:S(2)}) collective-permute-start(bf16[1,8]{1,0:T(2,128)(2,1)S(1)} %fusion.63), channel_id=1, source_target_pairs={{0,4},{4,8},{8,12},{1,5},{5,9},{9,13},{2,6},{6,10},{10,14},{3,7},{... | collective-permute-start | bytes 56 | tf_op jit(solution)/shard_map/while/body/eval_jaxpr/ppermute | solution.py:25
  306.3 3.9 %copy-start.5 = (bf16[512,8,128]{2,0,1:T(8,128)(2,1)S(1)}, bf16[512,8,128]{2,0,1:T(8,128)(2,1)}, u32[]{:S(2)}) copy-start(bf16[512,8,128]{2,0,1:T(8,128)(2,1)} %fusion.17) | copy-start | bytes 3145732
  306.3 3.9 %copy-start.6 = (pred[512,512]{0,1:T(8,128)(4,1)S(1)}, pred[512,512]{0,1:T(8,128)(4,1)}, u32[]{:S(2)}) copy-start(pred[512,512]{0,1:T(8,128)(4,1)} %fusion.34) | copy-start | bytes 786436
  310.2 3.8 %copy-start.4 = (bf16[1,512,1024]{1,2,0:T(8,128)(2,1)S(1)}, bf16[1,512,1024]{1,2,0:T(8,128)(2,1)}, u32[]{:S(2)}) copy-start(bf16[1,512,1024]{1,2,0:T(8,128)(2,1)} %slice.31) | copy-start | bytes 3145732
  310.2 3.8 %copy-start.7 = (pred[512,512]{0,1:T(8,128)(4,1)S(1)}, pred[512,512]{0,1:T(8,128)(4,1)}, u32[]{:S(2)}) copy-start(pred[512,512]{0,1:T(8,128)(4,1)} %iota_compare_fusion.1) | copy-start | bytes 786436
  320.9 18.3 %copy-start.3 = (bf16[1,512,2048]{2,1,0:T(8,128)(2,1)S(1)}, bf16[1,512,2048]{2,1,0:T(8,128)(2,1)}, u32[]{:S(2)}) copy-start(bf16[1,512,2048]{2,1,0:T(8,128)(2,1)} %param.9) | copy-start | bytes 6291460
Sparse Core Ops, SparseCore 0:
  8.9 104.4 all-gather.2
  114.9 76.2 all-gather.4
  327.4 11.7 reduce-scatter.1
